TPU v7x, 256 devices: a whole 4x4x8 slice. The times are simulated.
256 devices in a mesh: user: 16 (over z, core), item: 16 (over y, x).
Axes of the slice: x: 4, y: 4, z: 8, core: 2. Of those that a mesh axis runs over, the one named last changes fastest.
Arguments:
- ratings: bfloat16 [30720, 128, 128], P(('user', 'item')), may hold values from -6 to 6
- weights: bfloat16 [30720, 128, 128], P(('user', 'item')), may hold values from 0.19921875 to 2
- row_masks: int32 [30720, 4], P(('user', 'item')), may hold values from -2147483648 to 2147483646
- tile_users: int32 [30720], P(('user', 'item')), may hold values from 0 to 15
- tile_items: int32 [30720], P(('user', 'item')), may hold values from 0 to 15
- tile_counts: int32 [256], P(('user', 'item')), may hold values from 1 to 120
- users: float32 [32768, 128], P(('user', 'item')), may hold values from -1.8 to 1.8
- items: float32 [2048, 128], P('item'), may hold values from -1.8 to 1.8
Outputs:
- new_users: float32 [32768, 128], P(('user', 'item'))
- new_items: float32 [2048, 128], P('item')
All inputs are finite; a program needn't handle non-finite values.
Results may differ from a plain program's by a relative error of at most 0.002.
Values may be sent and summed in bfloat16 or wider, within the bound.
No kernel may reach another device: no remote copies, remote signals or barrier semaphores. Data moves between devices by JAX's collectives and lax.ppermute only.
A program may use at most 64 MiB of HBM per device.

v0:
```python
import jax
import jax.numpy as jnp
from jax import lax
from jax.sharding import PartitionSpec as P

STEPS = 2
STEP_SCALE = 4.0
DECAY_RATE = 0.02


def unpack_rows(packed, side):
    lanes = jnp.arange(side, dtype=jnp.int32)
    picked = packed[:, lanes // 32]
    return jnp.bitwise_and(jnp.right_shift(picked, lanes % 32), 1)


def tile_terms(user_panel, item_panel, tile_vals, tile_wts, packed, user_ids, item_ids, live_mask):
    side = tile_vals.shape[1]
    rowbits = unpack_rows(packed, side).astype(jnp.float32) * live_mask[:, None]
    weighted = tile_wts.astype(jnp.float32) * rowbits[:, :, None]
    user_rows = jnp.take(user_panel, user_ids, axis=0)
    item_rows = jnp.take(item_panel, item_ids, axis=0)
    predicted = jnp.einsum("tbr,tcr->tbc", user_rows, item_rows, preferred_element_type=jnp.float32)
    residual = (weighted * (tile_vals.astype(jnp.float32) - predicted)).astype(jnp.bfloat16)
    user_part = jnp.einsum("tbc,tcr->tbr", residual, item_rows, preferred_element_type=jnp.float32)
    item_part = jnp.einsum("tbc,tbr->tcr", residual, user_rows, preferred_element_type=jnp.float32)
    return (user_part, item_part, jnp.sum(weighted, axis=2), jnp.sum(weighted, axis=1))


def sweep(user_panel, item_panel, tiles, live_count, totals):
    per_block = 8
    blocks = (live_count + per_block - 1) // per_block

    def one_block(block, state):
        anchor = block * per_block

        def cut_block(array):
            return lax.dynamic_slice_in_dim(array, anchor, per_block, 0)

        tile_vals, tile_wts, packed, user_ids, item_ids = [cut_block(array) for array in tiles]
        slot_index = anchor + jnp.arange(per_block, dtype=jnp.int32)
        live_mask = (slot_index < live_count).astype(jnp.float32)
        user_part, item_part, user_rowsum, item_rowsum = tile_terms(
            user_panel, item_panel, tile_vals, tile_wts, packed, user_ids, item_ids, live_mask
        )
        user_sum, user_diag, item_sum, item_diag = state
        return (
            user_sum.at[user_ids].add(user_part),
            user_diag.at[user_ids].add(user_rowsum),
            item_sum.at[item_ids].add(item_part),
            item_diag.at[item_ids].add(item_rowsum),
        )

    return lax.fori_loop(0, blocks, one_block, totals)


def on_device(ratings, weights, row_masks, tile_users, tile_items, tile_counts, users, items):
    side = ratings.shape[1]
    rank = users.shape[1]
    count_here = tile_counts[0]
    own_tiles = (ratings, weights, row_masks, tile_users, tile_items)
    for iteration in range(STEPS):
        user_panel, item_panel = (
            lax.all_gather(users.astype(jnp.bfloat16), "item", axis=0, tiled=True),
            lax.all_gather(items.astype(jnp.bfloat16), "item", axis=0, tiled=True),
        )
        user_panel = user_panel.reshape(-1, side, rank)
        item_panel = item_panel.reshape(-1, side, rank)
        user_count = user_panel.shape[0]
        item_count = item_panel.shape[0]
        totals = (
            jnp.zeros((user_count, side, rank), jnp.float32),
            jnp.zeros((user_count, side), jnp.float32),
            jnp.zeros((item_count, side, rank), jnp.float32),
            jnp.zeros((item_count, side), jnp.float32),
        )
        user_sum, user_diag, item_sum, item_diag = sweep(
            user_panel, item_panel, own_tiles, count_here, totals
        )
        user_grad = user_sum.reshape(-1, rank)
        user_diag = user_diag.reshape(-1)
        item_grad = item_sum.reshape(-1, rank)
        item_diag = item_diag.reshape(-1)
        user_grad, user_diag, item_grad, item_diag = (
            lax.psum_scatter(user_grad, "item", scatter_dimension=0, tiled=True),
            lax.psum_scatter(user_diag, "item", scatter_dimension=0, tiled=True),
            lax.psum_scatter(item_grad, "item", scatter_dimension=0, tiled=True),
            lax.psum_scatter(item_diag, "item", scatter_dimension=0, tiled=True),
        )
        item_grad, item_diag = lax.psum((item_grad, item_diag), "user")
        user_weight = 2.0 * side + user_diag
        item_weight = 2.0 * side + item_diag
        users = users + STEP_SCALE * (user_grad / user_weight[:, None] - DECAY_RATE * users)
        items = items + STEP_SCALE * (item_grad / item_weight[:, None] - DECAY_RATE * items)
    return (users, items)


def solution(mesh):
    return jax.shard_map(
        on_device,
        mesh=mesh,
        in_specs=(
            P(("user", "item"), None, None),
            P(("user", "item"), None, None),
            P(("user", "item"), None),
            P(("user", "item")),
            P(("user", "item")),
            P(("user", "item")),
            P(("user", "item"), None),
            P("item", None),
        ),
        out_specs=(P(("user", "item"), None), P("item", None)),
        check_vma=False,
    )
```

profile of v0, /device:TPU:1, one launch (start us, length us, event | category | flops | bytes accessed | tf_op | source)
XLA Modules:
  0.0 1030.7 jit_solution(3896531610678982321)
XLA Ops:
  7.9 0.8 convert_element_type.88
  9.6 21.8 %all_gather.13 = bf16[2048,128]{1,0:T(8,128)(2,1)} all-gather(bf16[128,128]{1,0:T(8,128)(2,1)S(1)} %convert_element_type.89), channel_id=1, replica_groups=mesh['user'=16,'item'=16] {'item'}, dimensions={0}, use_global_device_ids=true | all-gather | bytes 557056 | tf_op jit(solution)/shard_map/all_gather | solution.py:65
  31.3 19.9 %all_gather.12 = bf16[2048,128]{1,0:T(8,128)(2,1)} all-gather(bf16[128,128]{1,0:T(8,128)(2,1)S(1)} %convert_element_type.88), channel_id=1, replica_groups=mesh['user'=16,'item'=16] {'item'}, dimensions={0}, use_global_device_ids=true | all-gather | bytes 557056 | tf_op jit(solution)/shard_map/all_gather | solution.py:64
  51.5 41.9 %while.36 = (s32[]{:T(128)}, f32[16,128,128]{2,1,0:T(8,128)S(1)}, f32[16,128]{1,0:T(8,128)S(1)}, f32[16,128,128]{2,1,0:T(8,128)S(1)}, f32[16,128]{1,0:T(8,128)S(...) while((s32[]{:T(128)}, f32[16,128,128]{2,1,0:T(8,128)S(1)}, ...), condition=%wide.region_7.9_spmd, body=%wide.region_0.8_spmd.sunk | while | flops 102769920 | bytes 7946063 | solution.py:54
  54.6 1.4 fusion.45
  57.2 1.6 gather_fusion.2
  58.9 1.6 gather_fusion.1
  60.5 1.4 fusion.43
  62.3 0.9 fusion.44
  63.2 1.2 scatter_fusion
  64.3 1.2 scatter_fusion.2
  68.5 1.4 fusion.45
  71.2 1.6 gather_fusion.2
  72.8 1.6 gather_fusion.1
  74.5 1.4 fusion.43
  76.2 0.9 fusion.44
  77.1 1.2 scatter_fusion
  78.3 1.2 scatter_fusion.2
  82.5 1.4 fusion.45
  85.1 1.6 gather_fusion.2
  86.8 1.6 gather_fusion.1
  88.4 1.4 fusion.43
  90.1 0.9 fusion.44
  91.1 1.2 scatter_fusion
  92.2 1.2 scatter_fusion.2
  93.4 1.0 copy-done.2
  95.3 1.3 dynamic-slice
  97.2 175.6 %all-reduce.5 = (f32[2048]{0:T(1024)S(1)}, f32[2048]{0:T(1024)S(1)}) all-reduce(f32[2048]{0:T(1024)S(1)} %bitcast.50, f32[2048]{0:T(1024)S(1)} %bitcast.49), channel_id=3, replica_groups=mesh['user'=16,'item'=16] {'item'}, use_global_device_ids=true, to_apply=%region_9.11.clone | all-reduce | flops 4096 | bytes 32768
  272.9 96.4 %psum.29 = f32[128]{0:T(128)S(1)} all-reduce(f32[128]{0:T(128)S(1)} %dynamic-slice.3), channel_id=1, replica_groups=mesh['user'=16,'item'=16] {'user'}, use_global_device_ids=true, to_apply=%region_13.15 | all-reduce | flops 128 | bytes 1024 | tf_op jit(solution)/shard_map/psum | solution.py:90
  369.5 58.9 %reduce-scatter.5.cloned.1.call-done = f32[128,128]{1,0:T(8,128)} async-done(((f32[2048,128]{1,0:T(8,128)}), f32[128,128]{1,0:T(8,128)}) %reduce-scatter.5.cloned.1.call-update) | async-done | bytes 65552 | tf_op jit(solution)/shard_map/reduce_scatter | solution.py:85
  428.5 0.9 fusion.20
  429.4 19.8 %all_gather.14 = bf16[2048,128]{1,0:T(8,128)(2,1)} all-gather(bf16[128,128]{1,0:T(8,128)(2,1)S(1)} %fusion.20), channel_id=1, replica_groups=mesh['user'=16,'item'=16] {'item'}, dimensions={0}, use_global_device_ids=true | all-gather | bytes 557056 | tf_op jit(solution)/shard_map/all_gather | solution.py:64
  449.2 82.0 %all-reduce.9.cloned.1.call-done = f32[128,128]{1,0:T(8,128)} async-done(((f32[128,128]{1,0:T(8,128)}), f32[128,128]{1,0:T(8,128)}) %all-reduce.9.cloned.1.call-update) | async-done | bytes 65552 | tf_op jit(solution)/shard_map/psum | solution.py:90
  531.2 0.9 fusion.21
  532.1 21.0 %all_gather.15 = bf16[2048,128]{1,0:T(8,128)(2,1)} all-gather(bf16[128,128]{1,0:T(8,128)(2,1)S(1)} %fusion.21), channel_id=1, replica_groups=mesh['user'=16,'item'=16] {'item'}, dimensions={0}, use_global_device_ids=true | all-gather | bytes 557056 | tf_op jit(solution)/shard_map/all_gather | solution.py:65
  553.3 41.9 %while.37 = (s32[]{:T(128)}, f32[16,128,128]{2,1,0:T(8,128)S(1)}, f32[16,128]{1,0:T(8,128)S(1)}, f32[16,128,128]{2,1,0:T(8,128)S(1)}, f32[16,128]{1,0:T(8,128)S(...) while((s32[]{:T(128)}, f32[16,128,128]{2,1,0:T(8,128)S(1)}, ...), condition=%wide.region_21.23_spmd, body=%wide.region_14.22_spmd.sunk | while | flops 102769920 | bytes 7946063 | solution.py:54
  556.4 1.4 fusion.52
  559.0 1.6 gather_fusion.5
  560.6 1.6 gather_fusion.4
  562.3 1.4 fusion.50
  564.0 0.9 fusion.51
  565.0 1.2 scatter_fusion.4
  566.1 1.2 scatter_fusion.6
  570.3 1.4 fusion.52
  572.9 1.6 gather_fusion.5
  574.6 1.6 gather_fusion.4
  576.2 1.4 fusion.50
  578.0 1.0 fusion.51
  578.9 1.2 scatter_fusion.4
  580.1 1.2 scatter_fusion.6
  584.3 1.4 fusion.52
  586.9 1.6 gather_fusion.5
  588.6 1.6 gather_fusion.4
  590.2 1.4 fusion.50
  592.0 1.0 fusion.51
  592.9 1.2 scatter_fusion.4
  594.1 1.2 scatter_fusion.6
  595.3 1.0 copy-done
  597.0 177.4 %all-reduce.4 = (f32[2048]{0:T(1024)S(1)}, f32[2048]{0:T(1024)S(1)}) all-reduce(f32[2048]{0:T(1024)S(1)} %bitcast.48, f32[2048]{0:T(1024)S(1)} %bitcast.47), channel_id=7, replica_groups=mesh['user'=16,'item'=16] {'item'}, use_global_device_ids=true, to_apply=%region_23.25.clone | all-reduce | flops 4096 | bytes 32768
  774.4 87.9 %psum.31 = f32[128]{0:T(128)S(1)} all-reduce(f32[128]{0:T(128)S(1)} %dynamic-slice.7), channel_id=1, replica_groups=mesh['user'=16,'item'=16] {'user'}, use_global_device_ids=true, to_apply=%region_27.29 | all-reduce | flops 128 | bytes 1024 | tf_op jit(solution)/shard_map/psum | solution.py:90
  862.4 57.2 %reduce-scatter.9.cloned.1.call-done = f32[128,128]{1,0:T(8,128)} async-done(((f32[2048,128]{1,0:T(8,128)}), f32[128,128]{1,0:T(8,128)}) %reduce-scatter.9.cloned.1.call-update) | async-done | bytes 65552 | tf_op jit(solution)/shard_map/reduce_scatter | solution.py:85
  919.6 1.6 multiply_add_fusion.1
  921.3 101.0 %all-reduce.11.cloned.1.call-done = f32[128,128]{1,0:T(8,128)} async-done(((f32[128,128]{1,0:T(8,128)}), f32[128,128]{1,0:T(8,128)}) %all-reduce.11.cloned.1.call-update) | async-done | bytes 65552 | tf_op jit(solution)/shard_map/psum | solution.py:90
  1022.3 1.6 multiply_add_fusion
  (163 shorter events, 30.1 us)
Async XLA Ops:
  7.2 362.3 %reduce-scatter.7.cloned.1.call-start = ((), (), s32[]{:S(2)}) async-start(), calls=%async_computation.5 | async-start | bytes 1114112 | tf_op jit(solution)/shard_map/reduce_scatter | solution.py:87
  51.5 377.0 %copy-start.4 = (f32[128,128]{1,0:T(8,128)S(1)}, f32[128,128]{1,0:T(8,128)}, u32[]{:S(2)}) copy-start(f32[128,128]{1,0:T(8,128)} %param.20) | copy-start | bytes 196612
  51.5 479.7 %copy-start.5 = (f32[128,128]{1,0:T(8,128)S(1)}, f32[128,128]{1,0:T(8,128)}, u32[]{:S(2)}) copy-start(f32[128,128]{1,0:T(8,128)} %param.21) | copy-start | bytes 196612
  53.8 8.2 copy-start.6
  53.8 8.2 copy-start.8
  53.8 8.2 copy-start.10
  67.7 8.2 copy-start.6
  67.7 8.2 copy-start.8
  67.7 8.2 copy-start.10
  81.7 8.2 copy-start.6
  81.7 8.2 copy-start.8
  81.7 8.2 copy-start.10
  93.4 1.0 copy-start.2
  93.4 1.4 copy-start.3
  94.5 334.0 %reduce-scatter.5.cloned.1.call-start = ((), (), s32[]{:S(2)}) async-start(), calls=%async_computation.4 | async-start | bytes 1114112 | tf_op jit(solution)/shard_map/reduce_scatter | solution.py:85
  95.2 435.9 %all-reduce.9.cloned.1.call-start = ((), (), s32[]{:S(2)}) async-start(), calls=%async_computation.6 | async-start | bytes 131072 | tf_op jit(solution)/shard_map/psum | solution.py:90
  369.4 183.7 %copy-start.13 = (f32[128]{0:T(128)}, f32[128]{0:T(128)S(1)}, u32[]{:S(2)}) copy-start(f32[128]{0:T(128)S(1)} %dynamic-slice_add_fusion.1) | copy-start | bytes 1540
  369.4 183.7 %copy-start.12 = (f32[128]{0:T(128)}, f32[128]{0:T(128)S(1)}, u32[]{:S(2)}) copy-start(f32[128]{0:T(128)S(1)} %broadcast_add_fusion.1) | copy-start | bytes 1540
  369.5 492.9 %reduce-scatter.11.cloned.1.call-start = ((), (), s32[]{:S(2)}) async-start(), calls=%async_computation.8 | async-start | bytes 1114112 | tf_op jit(solution)/shard_map/reduce_scatter | solution.py:87
  555.5 8.2 copy-start.7
  555.5 8.2 copy-start.9
  555.5 8.2 copy-start.11
  569.5 8.2 copy-start.7
  569.5 8.2 copy-start.9
  569.5 8.2 copy-start.11
  583.5 8.2 copy-start.7
  583.5 8.2 copy-start.9
  583.5 8.2 copy-start.11
  595.3 1.0 copy-start
  595.3 1.4 copy-start.1
  596.3 323.3 %reduce-scatter.9.cloned.1.call-start = ((), (), s32[]{:S(2)}) async-start(), calls=%async_computation.7 | async-start | bytes 1114112 | tf_op jit(solution)/shard_map/reduce_scatter | solution.py:85
  596.9 425.4 %all-reduce.11.cloned.1.call-start = ((), (), s32[]{:S(2)}) async-start(), calls=%async_computation.9 | async-start | bytes 131072 | tf_op jit(solution)/shard_map/psum | solution.py:90
Sparse Core Ops, SparseCore 0:
  94.6 252.5 reduce-scatter.6
  351.1 77.3 reduce-scatter.4
  430.8 100.3 all-reduce.8
  596.4 242.5 reduce-scatter.10
  842.4 77.2 reduce-scatter.8
  921.9 100.2 all-reduce.10
where the time goes:
time: 1040 us; the launch traced here: 1030 us
  blocking collectives  620 us (60%)
  waiting for transfers between devices  300 us (29%)
  other arithmetic  45.4 us (4%)
  local copies, waits for them, and re-layouts  32.9 us (3%)
  matrix products  15.8 us (2%)
  between operations  15.6 us (2%)
    unnamed x2, blocking collectives  353 us
    psum x2, blocking collectives, on_device(): item_grad, item_diag = lax.psum((item_grad, item_diag), 'user')  184 us
    psum x2, waiting for transfers between devices, on_device(): item_grad, item_diag = lax.psum((item_grad, item_diag), 'user')  183 us
    reduce_scatter x2, waiting for transfers between devices, on_device(): lax.psum_scatter(user_grad, 'item', scatter_dimension=0, tiled=True)  116 us
    all_gather x2, blocking collectives, on_device(): lax.all_gather(items.astype(jnp.bfloat16), 'item', axis=0, tiled=True)  42.7 us
    all_gather x2, blocking collectives, on_device(): lax.all_gather(users.astype(jnp.bfloat16), 'item', axis=0, tiled=True)  39.7 us
  transfers between devices with their start and end apart: 6, of which 4 were waited for; matrix products, arithmetic and copies ran while one was open for 0% of the time, Pallas kernels for 0%

commit v1 on v0

--- a/solution.py
+++ b/solution.py
@@ -61,7 +61,12 @@
     own_tiles = (ratings, weights, row_masks, tile_users, tile_items)
     for iteration in range(STEPS):
         user_panel, item_panel = (
-            lax.all_gather(users.astype(jnp.bfloat16), "item", axis=0, tiled=True),
+            jnp.concatenate(
+                lax.all_to_all(
+                    jnp.stack([users.astype(jnp.bfloat16)] * lax.axis_size("item")), "item", 0, 0
+                ),
+                axis=0,
+            ),
             lax.all_gather(items.astype(jnp.bfloat16), "item", axis=0, tiled=True),
         )
         user_panel = user_panel.reshape(-1, side, rank)

time: 1040 us -> 1010 us (0.971)
  blocking collectives: 620 us -> 564 us
  waiting for transfers between devices: 300 us -> 318 us
  starting transfers between devices: 0.24 us -> 12.1 us
    reduce_scatter x2, waiting for transfers between devices: 116 us -> 57.3 us  [on_device(): lax.psum_scatter(user_grad, 'item', scatter_dimension=0, tiled=True)]
    reduce_scatter x2, waiting for transfers between devices: 0.01 us -> 56.3 us  [on_device(): lax.psum_scatter(item_grad, 'item', scatter_dimension=0, tiled=True)]
    all_gather x2 -> x0, blocking collectives: 39.7 us -> none  [on_device(): lax.all_gather(users.astype(jnp.bfloat16), 'item', axis=0, tiled=True)]
    psum x2, waiting for transfers between devices: 183 us -> 204 us  [on_device(): item_grad, item_diag = lax.psum((item_grad, item_diag), 'user')]
    all_to_all x0 -> x2, starting transfers between devices: none -> 11.9 us  [on_device(): lax.all_to_all(jnp.stack([users.astype(jnp.bfloat16)] * lax.axis_size('it...]
  transfers between devices with their start and end apart: 6 -> 8, of which waited for: 4 -> 4; matrix products, arithmetic and copies ran while one was open for 0% -> 1% of each run, Pallas kernels for 0% -> 0%
where the time goes in v1:
time: 1010 us; the launch traced here: 1000 us
  blocking collectives  564 us (56%)
  waiting for transfers between devices  318 us (31%)
  other arithmetic  44.6 us (4%)
  local copies, waits for them, and re-layouts  34.7 us (3%)
  between operations  15.6 us (2%)
  matrix products  14 us (1%)
  starting transfers between devices  12.1 us (1%)
    unnamed x2, blocking collectives  345 us
    psum x2, waiting for transfers between devices, on_device(): item_grad, item_diag = lax.psum((item_grad, item_diag), 'user')  204 us
    psum x2, blocking collectives, on_device(): item_grad, item_diag = lax.psum((item_grad, item_diag), 'user')  175 us
    reduce_scatter x2, waiting for transfers between devices, on_device(): lax.psum_scatter(user_grad, 'item', scatter_dimension=0, tiled=True)  57.3 us
    reduce_scatter x2, waiting for transfers between devices, on_device(): lax.psum_scatter(item_grad, 'item', scatter_dimension=0, tiled=True)  56.3 us
    all_gather x2, blocking collectives, on_device(): lax.all_gather(items.astype(jnp.bfloat16), 'item', axis=0, tiled=True)  44 us
  transfers between devices with their start and end apart: 8, of which 4 were waited for; matrix products, arithmetic and copies ran while one was open for 1% of the time, Pallas kernels for 0%

profile of v1, /device:TPU:1, one launch (start us, length us, event | category | flops | bytes accessed | tf_op | source)
XLA Modules:
  0.0 1003.6 jit_solution(14753085723311536902)
XLA Ops:
  7.2 0.8 convert_element_type.88
  8.0 0.9 stack.4
  8.9 7.6 all-to-all-start
  17.3 0.8 convert_element_type.89
  18.1 23.0 %all_gather.6 = bf16[2048,128]{1,0:T(8,128)(2,1)} all-gather(bf16[128,128]{1,0:T(8,128)(2,1)S(1)} %convert_element_type.89), channel_id=1, replica_groups=mesh['user'=16,'item'=16] {'item'}, dimensions={0}, use_global_device_ids=true | all-gather | bytes 557056 | tf_op jit(solution)/shard_map/all_gather | solution.py:70
  41.4 39.1 %while.36 = (s32[]{:T(128)}, f32[16,128,128]{2,1,0:T(8,128)S(1)}, f32[16,128]{1,0:T(8,128)S(1)}, f32[16,128,128]{2,1,0:T(8,128)S(1)}, f32[16,128]{1,0:T(8,128)S(...) while((s32[]{:T(128)}, f32[16,128,128]{2,1,0:T(8,128)S(1)}, ...), condition=%wide.region_7.9_spmd, body=%wide.region_0.8_spmd.sunk | while | flops 102769920 | bytes 7945691 | solution.py:54
  44.4 1.4 fusion.45
  47.0 1.6 gather_fusion.2
  48.7 1.6 gather_fusion.1
  50.3 1.4 fusion.43
  52.3 1.0 scatter_fusion
  53.4 1.0 scatter_fusion.2
  57.4 1.4 fusion.45
  60.0 1.6 gather_fusion.2
  61.7 1.6 gather_fusion.1
  63.3 1.4 fusion.43
  65.3 1.0 scatter_fusion
  66.4 1.0 scatter_fusion.2
  70.4 1.4 fusion.45
  73.0 1.6 gather_fusion.2
  74.7 1.6 gather_fusion.1
  76.3 1.4 fusion.43
  78.4 1.0 scatter_fusion
  79.4 1.0 scatter_fusion.2
  80.5 1.0 copy-done.3
  82.3 1.3 dynamic-slice
  84.2 167.7 %all-reduce.5 = (f32[2048]{0:T(1024)S(1)}, f32[2048]{0:T(1024)S(1)}) all-reduce(f32[2048]{0:T(1024)S(1)} %bitcast.48, f32[2048]{0:T(1024)S(1)} %bitcast.47), channel_id=3, replica_groups=mesh['user'=16,'item'=16] {'item'}, use_global_device_ids=true, to_apply=%region_9.11.clone | all-reduce | flops 4096 | bytes 32768
  252.0 86.9 %psum.29 = f32[128]{0:T(128)S(1)} all-reduce(f32[128]{0:T(128)S(1)} %dynamic-slice.3), channel_id=1, replica_groups=mesh['user'=16,'item'=16] {'user'}, use_global_device_ids=true, to_apply=%region_13.15 | all-reduce | flops 128 | bytes 1024 | tf_op jit(solution)/shard_map/psum | solution.py:95
  338.9 0.9 fusion.20
  339.9 0.9 stack.5
  340.8 4.2 all-to-all-start.1
  345.1 56.3 %reduce-scatter.7.cloned.1.call-done = f32[128,128]{1,0:T(8,128)} async-done(((f32[2048,128]{1,0:T(8,128)}), f32[128,128]{1,0:T(8,128)}) %reduce-scatter.7.cloned.1.call-update) | async-done | bytes 65552 | tf_op jit(solution)/shard_map/reduce_scatter | solution.py:92
  401.5 102.5 %all-reduce.9.cloned.1.call-done = f32[128,128]{1,0:T(8,128)} async-done(((f32[128,128]{1,0:T(8,128)}), f32[128,128]{1,0:T(8,128)}) %all-reduce.9.cloned.1.call-update) | async-done | bytes 65552 | tf_op jit(solution)/shard_map/psum | solution.py:95
  504.0 0.9 fusion.21
  505.0 21.0 %all_gather.7 = bf16[2048,128]{1,0:T(8,128)(2,1)} all-gather(bf16[128,128]{1,0:T(8,128)(2,1)S(1)} %fusion.21), channel_id=1, replica_groups=mesh['user'=16,'item'=16] {'item'}, dimensions={0}, use_global_device_ids=true | all-gather | bytes 557056 | tf_op jit(solution)/shard_map/all_gather | solution.py:70
  526.2 41.9 %while.37 = (s32[]{:T(128)}, f32[16,128,128]{2,1,0:T(8,128)S(1)}, f32[16,128]{1,0:T(8,128)S(1)}, f32[16,128,128]{2,1,0:T(8,128)S(1)}, f32[16,128]{1,0:T(8,128)S(...) while((s32[]{:T(128)}, f32[16,128,128]{2,1,0:T(8,128)S(1)}, ...), condition=%wide.region_21.23_spmd, body=%wide.region_14.22_spmd.sunk | while | flops 102769920 | bytes 7946063 | solution.py:54
  529.2 1.4 fusion.52
  531.9 1.6 gather_fusion.5
  533.5 1.6 gather_fusion.4
  535.2 1.4 fusion.50
  536.9 1.0 fusion.51
  537.9 1.2 scatter_fusion.4
  539.0 1.2 scatter_fusion.6
  543.2 1.4 fusion.52
  545.8 1.6 gather_fusion.5
  547.5 1.6 gather_fusion.4
  549.1 1.4 fusion.50
  550.9 1.0 fusion.51
  551.8 1.2 scatter_fusion.4
  553.0 1.2 scatter_fusion.6
  557.2 1.4 fusion.52
  559.8 1.6 gather_fusion.5
  561.5 1.6 gather_fusion.4
  563.1 1.4 fusion.50
  564.8 1.0 fusion.51
  565.8 1.2 scatter_fusion.4
  567.0 1.2 scatter_fusion.6
  568.2 1.0 copy-done
  569.8 177.4 %all-reduce.4 = (f32[2048]{0:T(1024)S(1)}, f32[2048]{0:T(1024)S(1)}) all-reduce(f32[2048]{0:T(1024)S(1)} %bitcast.46, f32[2048]{0:T(1024)S(1)} %bitcast.45), channel_id=7, replica_groups=mesh['user'=16,'item'=16] {'item'}, use_global_device_ids=true, to_apply=%region_23.25.clone | all-reduce | flops 4096 | bytes 32768
  747.3 87.8 %psum.31 = f32[128]{0:T(128)S(1)} all-reduce(f32[128]{0:T(128)S(1)} %dynamic-slice.7), channel_id=1, replica_groups=mesh['user'=16,'item'=16] {'user'}, use_global_device_ids=true, to_apply=%region_27.29 | all-reduce | flops 128 | bytes 1024 | tf_op jit(solution)/shard_map/psum | solution.py:95
  835.3 57.3 %reduce-scatter.9.cloned.1.call-done = f32[128,128]{1,0:T(8,128)} async-done(((f32[2048,128]{1,0:T(8,128)}), f32[128,128]{1,0:T(8,128)}) %reduce-scatter.9.cloned.1.call-update) | async-done | bytes 65552 | tf_op jit(solution)/shard_map/reduce_scatter | solution.py:90
  892.5 1.6 multiply_add_fusion.1
  894.1 101.0 %all-reduce.11.cloned.1.call-done = f32[128,128]{1,0:T(8,128)} async-done(((f32[128,128]{1,0:T(8,128)}), f32[128,128]{1,0:T(8,128)}) %all-reduce.11.cloned.1.call-update) | async-done | bytes 65552 | tf_op jit(solution)/shard_map/psum | solution.py:95
  995.1 1.6 multiply_add_fusion
  (149 shorter events, 30.1 us)
Async XLA Ops:
  8.9 32.2 %all-to-all-start = ((bf16[16,128,128]{2,1,0:T(8,128)(2,1)}), bf16[16,128,128]{2,1,0:T(8,128)(2,1)}, u32[]{:S(2)}, u32[]{:S(2)}) async-start(bf16[16,128,128]{2,1,0:T(8,128)(2,1)} %stack.4), calls=%async_computation | async-start | bytes 1048576 | tf_op jit(solution)/shard_map/all_to_all | solution.py:65
  16.6 322.4 %reduce-scatter.5.cloned.1.call-start = ((), (), s32[]{:S(2)}) async-start(), calls=%async_computation.6 | async-start | bytes 1114112 | tf_op jit(solution)/shard_map/reduce_scatter | solution.py:90
  41.4 297.6 %copy-start.4 = (f32[128,128]{1,0:T(8,128)S(1)}, f32[128,128]{1,0:T(8,128)}, u32[]{:S(2)}) copy-start(f32[128,128]{1,0:T(8,128)} %param.20) | copy-start | bytes 196612
  80.5 1.0 copy-start.3
  80.5 1.4 copy-start.2
  80.5 423.6 %copy-start.5 = (f32[128,128]{1,0:T(8,128)S(1)}, f32[128,128]{1,0:T(8,128)}, u32[]{:S(2)}) copy-start(f32[128,128]{1,0:T(8,128)} %param.21) | copy-start | bytes 196612
  81.5 319.9 %reduce-scatter.7.cloned.1.call-start = ((), (), s32[]{:S(2)}) async-start(), calls=%async_computation.7 | async-start | bytes 1114112 | tf_op jit(solution)/shard_map/reduce_scatter | solution.py:92
  338.9 187.0 %copy-start.9 = (f32[128]{0:T(128)}, f32[128]{0:T(128)S(1)}, u32[]{:S(2)}) copy-start(f32[128]{0:T(128)S(1)} %dynamic-slice_add_fusion.1) | copy-start | bytes 1540
  340.8 185.2 %all-to-all-start.1 = ((bf16[16,128,128]{2,1,0:T(8,128)(2,1)}), bf16[16,128,128]{2,1,0:T(8,128)(2,1)}, u32[]{:S(2)}, u32[]{:S(2)}) async-start(bf16[16,128,128]{2,1,0:T(8,128)(2,1)} %stack.5), calls=%async_computation.2 | async-start | bytes 1048576 | tf_op jit(solution)/shard_map/all_to_all | solution.py:65
  345.0 159.0 %all-reduce.9.cloned.1.call-start = ((), (), s32[]{:S(2)}) async-start(), calls=%async_computation.8 | async-start | bytes 131072 | tf_op jit(solution)/shard_map/psum | solution.py:95
  401.4 433.8 %reduce-scatter.11.cloned.1.call-start = ((), (), s32[]{:S(2)}) async-start(), calls=%async_computation.10 | async-start | bytes 1114112 | tf_op jit(solution)/shard_map/reduce_scatter | solution.py:92
  401.5 124.5 %copy-start.10 = (f32[128]{0:T(128)}, f32[128]{0:T(128)S(1)}, u32[]{:S(2)}) copy-start(f32[128]{0:T(128)S(1)} %broadcast_add_fusion.1) | copy-start | bytes 1540
  528.4 8.2 copy-start.6
  528.4 8.2 copy-start.7
  528.4 8.2 copy-start.8
  542.4 8.2 copy-start.6
  542.4 8.2 copy-start.7
  542.4 8.2 copy-start.8
  556.4 8.2 copy-start.6
  556.4 8.2 copy-start.7
  556.4 8.2 copy-start.8
  568.1 1.0 copy-start
  568.1 1.4 copy-start.1
  569.2 323.3 %reduce-scatter.9.cloned.1.call-start = ((), (), s32[]{:S(2)}) async-start(), calls=%async_computation.9 | async-start | bytes 1114112 | tf_op jit(solution)/shard_map/reduce_scatter | solution.py:90
  569.8 425.3 %all-reduce.11.cloned.1.call-start = ((), (), s32[]{:S(2)}) async-start(), calls=%async_computation.11 | async-start | bytes 131072 | tf_op jit(solution)/shard_map/psum | solution.py:95
Sparse Core Ops, SparseCore 0:
  81.6 235.6 reduce-scatter.4
  321.3 80.0 reduce-scatter.6
  403.7 100.2 all-reduce.8
  569.3 242.5 reduce-scatter.10
  815.2 77.2 reduce-scatter.8
  894.8 100.2 all-reduce.10
